TPU v7x, 32 devices: a whole 2x2x4 slice. The times are simulated.
32 devices in a mesh: parts: 2 (over y), row: 2 (over x), col: 2 (over core), layer: 4 (over z).
Axes of the slice: x: 2, y: 2, z: 4, core: 2. Of those that a mesh axis runs over, the one named last changes fastest.
Arguments:
- dosages: bfloat16 [4096, 2048], P(('layer', 'col'), ('parts', 'row')), parts along dimension 1, may hold values from -6 to 6
- expression: bfloat16 [4096, 16384], P('layer', ('col', 'row')), may hold values from -6 to 6
Outputs:
- zscores: float32 [2048, 16384], P(('parts', 'row', 'layer'), 'col'), parts along dimension 0
There are 2 independent parts, one for each index of `parts`. A program takes and returns all parts, laid end to end along the dimension named above; an argument that names none is the same for every part. Nothing has to cross between parts.
All inputs are finite; a program needn't handle non-finite values.
Results may differ from a plain program's by a relative error of at most 0.0003.
Values may be sent and summed in bfloat16 or wider, within the bound.
No kernel may reach another device: no remote copies, remote signals or barrier semaphores. Data moves between devices by JAX's collectives and lax.ppermute only.
A program may use at most 128 MiB of HBM per device.

v0:
```python
import math
import jax
import jax.numpy as jnp
from jax import lax
from jax.sharding import PartitionSpec as P


def contract(left_rows, right_rows):
    return lax.dot_general(
        left_rows, right_rows, (((0,), (0,)), ((), ())), preferred_element_type=jnp.float32
    )


def full_dosages(local):
    samples = lax.all_gather(local, "col", axis=0, tiled=True)
    return lax.all_gather(samples, "row", axis=1, tiled=True)


def pick(d4, index):
    block = lax.dynamic_index_in_dim(d4, index, axis=2, keepdims=False)
    return block.reshape(block.shape[0], -1)


def on_device(dosages, expression):
    layers = lax.axis_size("layer")
    rows = lax.axis_size("row")
    layer = lax.axis_index("layer")
    row = lax.axis_index("row")
    factor = 1.0 / math.sqrt(dosages.shape[0] * lax.axis_size("col") * layers)
    samples, width = expression.shape
    block = dosages.shape[1] // layers
    half = layers // 2
    inward = [(0, 1), (layers - 1, layers - 2)]
    across = [(half - 1, half), (half, half - 1)]
    outward = [(1, 0), (layers - 2, layers - 1)]
    dosages_in = lax.ppermute(dosages, "layer", inward)
    own4 = full_dosages(dosages).reshape(samples, rows, layers, block)
    out4 = full_dosages(dosages_in).reshape(samples, rows, layers, block)
    is_left = layer < half
    outer = jnp.where(is_left, 0, layers - 1)
    near = layers - 1 - layer
    far = layers - 1 - outer
    own_far = jnp.concatenate([pick(own4, near), pick(own4, far)], axis=1)
    out_far = jnp.concatenate([pick(out4, near), pick(out4, far)], axis=1)
    own_here = pick(own4, layer)
    out_here = pick(out4, layer)
    own_outer = pick(own4, outer)
    stripe = rows * block
    chunks = max(1, min(8, width // 512))
    step = width // chunks
    output = jnp.zeros((block, rows * width), jnp.float32)
    for k in range(chunks):
        mine = expression[:, k * step : (k + 1) * step]
        theirs = lax.ppermute(mine, "layer", inward)
        sent = contract(own_far, mine) + contract(out_far, theirs)
        got = lax.ppermute(sent, "layer", across)
        to_outer = contract(own_outer, mine) + got[stripe:]
        from_inner = lax.ppermute(to_outer, "layer", outward)
        final = contract(own_here, mine) + contract(out_here, theirs) + got[:stripe] + from_inner
        final = (final * factor).reshape(rows, block, step)
        for shift in range(rows):
            target = (row + shift) % rows
            piece = lax.dynamic_index_in_dim(final, target, axis=0, keepdims=False)
            if shift:
                pairs = [(source, (source + shift) % rows) for source in range(rows)]
                piece = lax.ppermute(piece, "row", pairs)
            source = (row - shift) % rows
            output = lax.dynamic_update_slice_in_dim(output, piece, source * width + k * step, 1)
    return output


def solution(mesh):
    return jax.shard_map(
        on_device,
        mesh=mesh,
        in_specs=(P(("layer", "col"), ("parts", "row")), P("layer", ("col", "row"))),
        out_specs=P(("parts", "row", "layer"), "col"),
        check_vma=False,
    )
```

profile of v0, /device:TPU:0, one launch (start us, length us, event | category | flops | bytes accessed | tf_op | source)
XLA Modules:
  0.0 399.0 jit_solution(11919725374042339640)
XLA Ops:
  6.5 2.0 copy.3
  8.7 5.0 %collective-permute-start = (bf16[512,512]{0,1:T(8,128)(2,1)}, bf16[512,512]{0,1:T(8,128)(2,1)S(1)}, u32[]{:S(2)}, u32[]{:S(2)}) collective-permute-start(bf16[512,512]{0,1:T(8,128)(2,1)} %copy.3), channel_id=1, source_target_pairs={{0,1},{3,2},{4,5},{7,6},{8,9},{11,10},{12,13},{15,14},{16,17},{19,... | collective-permute-start | bytes 1572872 | tf_op jit(solution)/shard_map/ppermute | solution.py:36
  13.7 11.4 %collective-permute-done = bf16[512,512]{0,1:T(8,128)(2,1)S(1)} collective-permute-done((bf16[512,512]{0,1:T(8,128)(2,1)}, bf16[512,512]{0,1:T(8,128)(2,1)S(1)}, u32[]{:S(2)}, u32[]{:S(2)}) %collective-permute-start) | collective-permute-done | bytes 524320 | tf_op jit(solution)/shard_map/ppermute | solution.py:36
  26.7 9.4 %all-gather.9.cloned.1.call-done = bf16[1024,512]{0,1:T(8,128)(2,1)} async-done(((bf16[512,512]{0,1:T(8,128)(2,1)}), bf16[1024,512]{0,1:T(8,128)(2,1)}) %all-gather.9.cloned.1.call-update) | async-done | bytes 1048592 | tf_op jit(solution)/shard_map/all_gather | solution.py:15
  36.2 6.3 %fusion.88 = (bf16[1024,512]{1,0:T(8,128)(2,1)}, bf16[1024,512]{1,0:T(8,128)(2,1)}, bf16[1024,512]{1,0:T(8,128)(2,1)}, bf16[1024,512]{1,0:T(8,128)(2,1)}, bf16[1...) fusion(bf16[1024,4096]{1,0:T(8,128)(2,1)} %param.3), kind=kLoop, calls=%fused_computation.129 | loop fusion | bytes 16777216 | tf_op jit(solution)/shard_map/slice | solution.py:53
  42.4 3.7 collective-permute-start.21
  46.2 1.4 collective-permute-start.17
  47.5 2.3 collective-permute-start.13
  49.8 1.3 collective-permute-start.9
  51.1 2.3 collective-permute-start.5
  53.4 18.5 %all-gather.7.cloned.1.call-done = bf16[1024,1024]{0,1:T(8,128)(2,1)} async-done(((bf16[1024,512]{0,1:T(8,128)(2,1)}), bf16[1024,1024]{0,1:T(8,128)(2,1)}) %all-gather.7.cloned.1.call-update) | async-done | bytes 2097168 | tf_op jit(solution)/shard_map/all_gather | solution.py:16
  72.0 34.5 %all-gather.11.cloned.1.call-done = bf16[1024,1024]{0,1:T(8,128)(2,1)} async-done(((bf16[1024,512]{0,1:T(8,128)(2,1)}), bf16[1024,1024]{0,1:T(8,128)(2,1)}) %all-gather.11.cloned.1.call-update) | async-done | bytes 2097168 | tf_op jit(solution)/shard_map/all_gather | solution.py:16
  106.5 2.6 constant_dynamic-slice_fusion.5
  109.1 2.1 fusion.42
  111.2 1.9 fusion.50
  116.4 3.4 collective-permute-start.1
  120.6 1.4 collective-permute-start.25
  122.7 1.4 collective-permute-start.29
  124.1 1.9 convolution_add_fusion.4
  126.0 11.3 %collective-permute-done.9 = bf16[1024,512]{1,0:T(8,128)(2,1)S(1)} collective-permute-done((bf16[1024,512]{1,0:T(8,128)(2,1)}, bf16[1024,512]{1,0:T(8,128)(2,1)S(1)}, u32[]{:S(2)}, u32[]{:S(2)}) %collective-permute-start.9) | collective-permute-done | bytes 1048608 | tf_op jit(solution)/shard_map/ppermute | solution.py:54
  141.7 18.2 %collective-permute-done.5 = bf16[1024,512]{1,0:T(8,128)(2,1)} collective-permute-done((bf16[1024,512]{1,0:T(8,128)(2,1)}, bf16[1024,512]{1,0:T(8,128)(2,1)}, u32[]{:S(2)}, u32[]{:S(2)}) %collective-permute-start.5) | collective-permute-done | bytes 1048608 | tf_op jit(solution)/shard_map/ppermute | solution.py:54
  160.6 1.9 convolution_add_fusion.6
  162.5 19.7 %collective-permute-done.1 = bf16[1024,512]{1,0:T(8,128)(2,1)S(1)} collective-permute-done((bf16[1024,512]{1,0:T(8,128)(2,1)S(1)}, bf16[1024,512]{1,0:T(8,128)(2,1)S(1)}, u32[]{:S(2)}, u32[]{:S(2)}) %collective-permute-start.1) | collective-permute-done | bytes 1048608 | tf_op jit(solution)/shard_map/ppermute | solution.py:54
  183.6 21.0 %collective-permute-done.25 = bf16[1024,512]{1,0:T(8,128)(2,1)S(1)} collective-permute-done((bf16[1024,512]{1,0:T(8,128)(2,1)S(1)}, bf16[1024,512]{1,0:T(8,128)(2,1)S(1)}, u32[]{:S(2)}, u32[]{:S(2)}) %collective-permute-start.25) | collective-permute-done | bytes 1048608 | tf_op jit(solution)/shard_map/ppermute | solution.py:54
  206.3 20.2 %collective-permute-done.29 = bf16[1024,512]{1,0:T(8,128)(2,1)S(1)} collective-permute-done((bf16[1024,512]{1,0:T(8,128)(2,1)S(1)}, bf16[1024,512]{1,0:T(8,128)(2,1)S(1)}, u32[]{:S(2)}, u32[]{:S(2)}) %collective-permute-start.29) | collective-permute-done | bytes 1048608 | tf_op jit(solution)/shard_map/ppermute | solution.py:54
  233.3 1.3 collective-permute-start.23
  235.0 1.3 collective-permute-start.19
  236.8 1.3 collective-permute-start.15
  238.6 1.3 collective-permute-start.7
  240.3 1.3 collective-permute-start.3
  242.1 70.3 %collective-permute-done.7 = f32[256,512]{1,0:T(8,128)S(1)} collective-permute-done((f32[256,512]{1,0:T(8,128)S(1)}, f32[256,512]{1,0:T(8,128)S(1)}, u32[]{:S(2)}, u32[]{:S(2)}) %collective-permute-start.7) | collective-permute-done | bytes 524320 | tf_op jit(solution)/shard_map/ppermute | solution.py:58
  312.4 1.3 collective-permute-start.11
  313.7 1.7 fusion.21
  315.4 21.5 %collective-permute-done.3 = f32[256,512]{1,0:T(8,128)S(1)} collective-permute-done((f32[256,512]{1,0:T(8,128)S(1)}, f32[256,512]{1,0:T(8,128)S(1)}, u32[]{:S(2)}, u32[]{:S(2)}) %collective-permute-start.3) | collective-permute-done | bytes 524320 | tf_op jit(solution)/shard_map/ppermute | solution.py:58
  338.7 1.3 collective-permute-start.31
  340.0 1.7 fusion.17
  341.7 6.4 %collective-permute-done.11 = f32[256,512]{1,0:T(8,128)S(1)} collective-permute-done((f32[256,512]{1,0:T(8,128)S(1)}, f32[256,512]{1,0:T(8,128)S(1)}, u32[]{:S(2)}, u32[]{:S(2)}) %collective-permute-start.11) | collective-permute-done | bytes 524320 | tf_op jit(solution)/shard_map/ppermute | solution.py:58
  348.1 1.5 collective-permute-start.4
  351.3 1.5 collective-permute-start.12
  353.4 6.0 %collective-permute-done.27 = f32[256,512]{1,0:T(8,128)S(1)} collective-permute-done((f32[256,512]{1,0:T(8,128)S(1)}, f32[256,512]{1,0:T(8,128)S(1)}, u32[]{:S(2)}, u32[]{:S(2)}) %collective-permute-start.27) | collective-permute-done | bytes 524320 | tf_op jit(solution)/shard_map/ppermute | solution.py:58
  359.4 1.5 collective-permute-start.16
  361.3 7.3 %collective-permute-done.31 = f32[256,512]{1,0:T(8,128)S(1)} collective-permute-done((f32[256,512]{1,0:T(8,128)S(1)}, f32[256,512]{1,0:T(8,128)S(1)}, u32[]{:S(2)}, u32[]{:S(2)}) %collective-permute-start.31) | collective-permute-done | bytes 524320 | tf_op jit(solution)/shard_map/ppermute | solution.py:58
  368.6 1.5 collective-permute-start.20
  371.7 1.5 collective-permute-start.28
  374.1 3.6 collective-permute-done.20
  377.8 5.6 %collective-permute-done.24 = f32[128,512]{1,0:T(8,128)S(1)} collective-permute-done((f32[128,512]{1,0:T(8,128)S(1)}, f32[128,512]{1,0:T(8,128)S(1)}, u32[]{:S(2)}, u32[]{:S(2)}) %collective-permute-start.24) | collective-permute-done | bytes 262176 | tf_op jit(solution)/shard_map/ppermute | solution.py:66
  383.4 5.5 %collective-permute-done.28 = f32[128,512]{1,0:T(8,128)S(1)} collective-permute-done((f32[128,512]{1,0:T(8,128)S(1)}, f32[128,512]{1,0:T(8,128)S(1)}, u32[]{:S(2)}, u32[]{:S(2)}) %collective-permute-start.28) | collective-permute-done | bytes 262176 | tf_op jit(solution)/shard_map/ppermute | solution.py:66
  389.0 2.7 collective-permute-done.32
  (113 shorter events, 30.9 us)
Async XLA Ops:
  6.5 19.4 %all-gather.5.cloned.1.call-start = ((), (), s32[]{:S(2)}) async-start(), calls=%async_computation | async-start | bytes 1572864 | tf_op jit(solution)/shard_map/all_gather | solution.py:15
  8.6 27.5 %all-gather.9.cloned.1.call-start = ((), (), s32[]{:S(2)}) async-start(), calls=%async_computation.2 | async-start | bytes 1572864 | tf_op jit(solution)/shard_map/all_gather | solution.py:15
  8.7 16.4 %collective-permute-start = (bf16[512,512]{0,1:T(8,128)(2,1)}, bf16[512,512]{0,1:T(8,128)(2,1)S(1)}, u32[]{:S(2)}, u32[]{:S(2)}) collective-permute-start(bf16[512,512]{0,1:T(8,128)(2,1)} %copy.3), channel_id=1, source_target_pairs={{0,1},{3,2},{4,5},{7,6},{8,9},{11,10},{12,13},{15,14},{16,17},{19,... | collective-permute-start | bytes 1572872 | tf_op jit(solution)/shard_map/ppermute | solution.py:36
  25.1 0.8 copy-start.4
  25.9 46.1 %all-gather.7.cloned.1.call-start = ((), (), s32[]{:S(2)}) async-start(), calls=%async_computation.1 | async-start | bytes 3145728 | tf_op jit(solution)/shard_map/all_gather | solution.py:16
  26.6 79.9 %all-gather.11.cloned.1.call-start = ((), (), s32[]{:S(2)}) async-start(), calls=%async_computation.3 | async-start | bytes 3145728 | tf_op jit(solution)/shard_map/all_gather | solution.py:16
  42.4 73.9 %collective-permute-start.21 = (bf16[1024,512]{1,0:T(8,128)(2,1)}, bf16[1024,512]{1,0:T(8,128)(2,1)S(1)}, u32[]{:S(2)}, u32[]{:S(2)}) collective-permute-start(bf16[1024,512]{1,0:T(8,128)(2,1)} %get-tuple-element.6), channel_id=1, source_target_pairs={{0,1},{3,2},{4,5},{7,6},{8,9},{11,10},{12,13},{15,14},{16,17},{19,... | collective-permute-start | bytes 3145736 | tf_op jit(solution)/shard_map/ppermute | solution.py:54
  46.2 74.4 %collective-permute-start.17 = (bf16[1024,512]{1,0:T(8,128)(2,1)}, bf16[1024,512]{1,0:T(8,128)(2,1)S(1)}, u32[]{:S(2)}, u32[]{:S(2)}) collective-permute-start(bf16[1024,512]{1,0:T(8,128)(2,1)} %get-tuple-element.7), channel_id=1, source_target_pairs={{0,1},{3,2},{4,5},{7,6},{8,9},{11,10},{12,13},{15,14},{16,17},{19,... | collective-permute-start | bytes 3145736 | tf_op jit(solution)/shard_map/ppermute | solution.py:54
  47.5 75.2 %collective-permute-start.13 = (bf16[1024,512]{1,0:T(8,128)(2,1)}, bf16[1024,512]{1,0:T(8,128)(2,1)}, u32[]{:S(2)}, u32[]{:S(2)}) collective-permute-start(bf16[1024,512]{1,0:T(8,128)(2,1)} %get-tuple-element.8), channel_id=1, source_target_pairs={{0,1},{3,2},{4,5},{7,6},{8,9},{11,10},{12,13},{15,14},{16,17},{19,... | collective-permute-start | bytes 3145736 | tf_op jit(solution)/shard_map/ppermute | solution.py:54
  49.8 87.6 %collective-permute-start.9 = (bf16[1024,512]{1,0:T(8,128)(2,1)}, bf16[1024,512]{1,0:T(8,128)(2,1)S(1)}, u32[]{:S(2)}, u32[]{:S(2)}) collective-permute-start(bf16[1024,512]{1,0:T(8,128)(2,1)} %get-tuple-element.9), channel_id=1, source_target_pairs={{0,1},{3,2},{4,5},{7,6},{8,9},{11,10},{12,13},{15,14},{16,17},{19,... | collective-permute-start | bytes 3145736 | tf_op jit(solution)/shard_map/ppermute | solution.py:54
  51.1 108.7 %collective-permute-start.5 = (bf16[1024,512]{1,0:T(8,128)(2,1)}, bf16[1024,512]{1,0:T(8,128)(2,1)}, u32[]{:S(2)}, u32[]{:S(2)}) collective-permute-start(bf16[1024,512]{1,0:T(8,128)(2,1)} %get-tuple-element.10), channel_id=1, source_target_pairs={{0,1},{3,2},{4,5},{7,6},{8,9},{11,10},{12,13},{15,14},{16,17},{19,... | collective-permute-start | bytes 3145736 | tf_op jit(solution)/shard_map/ppermute | solution.py:54
  106.5 6.6 %slice-start = ((s8[8388608]{0:T(1024)(128)(4,1)}), s8[4194304]{0:T(1024)(128)(4,1)S(1)}, s32[]{:S(2)}) async-start(s8[8388608]{0:T(1024)(128)(4,1)} %bitcast.105), calls=%async_computation.4 | async-start | bytes 8388608
  109.1 4.1 %slice-start.1 = ((s8[8388608]{0:T(1024)(128)(4,1)}), s8[4194304]{0:T(1024)(128)(4,1)S(1)}, s32[]{:S(2)}) async-start(s8[8388608]{0:T(1024)(128)(4,1)} %bitcast.105), calls=%async_computation.5 | async-start | bytes 8388608
  114.8 1.6 copy-start.3
  115.9 4.7 %copy-start.2 = (bf16[1024,512]{1,0:T(8,128)(2,1)S(1)}, bf16[1024,512]{1,0:T(8,128)(2,1)}, u32[]{:S(2)}) copy-start(bf16[1024,512]{1,0:T(8,128)(2,1)} %get-tuple-element.12) | copy-start | bytes 3145732
  116.4 65.8 %collective-permute-start.1 = (bf16[1024,512]{1,0:T(8,128)(2,1)S(1)}, bf16[1024,512]{1,0:T(8,128)(2,1)S(1)}, u32[]{:S(2)}, u32[]{:S(2)}) collective-permute-start(bf16[1024,512]{1,0:T(8,128)(2,1)S(1)} %copy-done.3), channel_id=1, source_target_pairs={{0,1},{3,2},{4,5},{7,6},{8,9},{11,10},{12,13},{15,14},{16,17},{19,... | collective-permute-start | bytes 3145736 | tf_op jit(solution)/shard_map/ppermute | solution.py:54
  119.8 2.9 copy-start.1
  120.6 84.1 %collective-permute-start.25 = (bf16[1024,512]{1,0:T(8,128)(2,1)S(1)}, bf16[1024,512]{1,0:T(8,128)(2,1)S(1)}, u32[]{:S(2)}, u32[]{:S(2)}) collective-permute-start(bf16[1024,512]{1,0:T(8,128)(2,1)S(1)} %copy-done.2), channel_id=1, source_target_pairs={{0,1},{3,2},{4,5},{7,6},{8,9},{11,10},{12,13},{15,14},{16,17},{19,... | collective-permute-start | bytes 3145736 | tf_op jit(solution)/shard_map/ppermute | solution.py:54
  122.7 103.7 %collective-permute-start.29 = (bf16[1024,512]{1,0:T(8,128)(2,1)S(1)}, bf16[1024,512]{1,0:T(8,128)(2,1)S(1)}, u32[]{:S(2)}, u32[]{:S(2)}) collective-permute-start(bf16[1024,512]{1,0:T(8,128)(2,1)S(1)} %copy-done.1), channel_id=1, source_target_pairs={{0,1},{3,2},{4,5},{7,6},{8,9},{11,10},{12,13},{15,14},{16,17},{19,... | collective-permute-start | bytes 3145736 | tf_op jit(solution)/shard_map/ppermute | solution.py:54
  137.4 92.3 %collective-permute-start.22 = (f32[512,512]{1,0:T(8,128)S(1)}, f32[512,512]{1,0:T(8,128)S(1)}, u32[]{:S(2)}, u32[]{:S(2)}) collective-permute-start(f32[512,512]{1,0:T(8,128)S(1)} %convolution_add_fusion.2), channel_id=1, source_target_pairs={{1,2},{2,1},{5,6},{6,5},{9,10},{10,9},{13,14},{14,13},{17,18},{18,... | collective-permute-start | bytes 3145736 | tf_op jit(solution)/shard_map/ppermute | solution.py:56
  159.8 71.1 %collective-permute-start.18 = (f32[512,512]{1,0:T(8,128)S(1)}, f32[512,512]{1,0:T(8,128)S(1)}, u32[]{:S(2)}, u32[]{:S(2)}) collective-permute-start(f32[512,512]{1,0:T(8,128)S(1)} %convolution_add_fusion.3), channel_id=1, source_target_pairs={{1,2},{2,1},{5,6},{6,5},{9,10},{10,9},{13,14},{14,13},{17,18},{18,... | collective-permute-start | bytes 3145736 | tf_op jit(solution)/shard_map/ppermute | solution.py:56
  182.2 49.9 %collective-permute-start.14 = (f32[512,512]{1,0:T(8,128)S(1)}, f32[512,512]{1,0:T(8,128)S(1)}, u32[]{:S(2)}, u32[]{:S(2)}) collective-permute-start(f32[512,512]{1,0:T(8,128)S(1)} %convolution_add_fusion.4), channel_id=1, source_target_pairs={{1,2},{2,1},{5,6},{6,5},{9,10},{10,9},{13,14},{14,13},{17,18},{18,... | collective-permute-start | bytes 3145736 | tf_op jit(solution)/shard_map/ppermute | solution.py:56
  204.7 28.6 %collective-permute-start.10 = (f32[512,512]{1,0:T(8,128)S(1)}, f32[512,512]{1,0:T(8,128)S(1)}, u32[]{:S(2)}, u32[]{:S(2)}) collective-permute-start(f32[512,512]{1,0:T(8,128)S(1)} %convolution_add_fusion.5), channel_id=1, source_target_pairs={{1,2},{2,1},{5,6},{6,5},{9,10},{10,9},{13,14},{14,13},{17,18},{18,... | collective-permute-start | bytes 3145736 | tf_op jit(solution)/shard_map/ppermute | solution.py:56
  226.5 8.6 %collective-permute-start.6 = (f32[512,512]{1,0:T(8,128)S(1)}, f32[512,512]{1,0:T(8,128)S(1)}, u32[]{:S(2)}, u32[]{:S(2)}) collective-permute-start(f32[512,512]{1,0:T(8,128)S(1)} %convolution_add_fusion.6), channel_id=1, source_target_pairs={{1,2},{2,1},{5,6},{6,5},{9,10},{10,9},{13,14},{14,13},{17,18},{18,... | collective-permute-start | bytes 3145736 | tf_op jit(solution)/shard_map/ppermute | solution.py:56
  229.7 7.1 %collective-permute-start.2 = (f32[512,512]{1,0:T(8,128)S(1)}, f32[512,512]{1,0:T(8,128)S(1)}, u32[]{:S(2)}, u32[]{:S(2)}) collective-permute-start(f32[512,512]{1,0:T(8,128)S(1)} %convolution_add_fusion.7), channel_id=1, source_target_pairs={{1,2},{2,1},{5,6},{6,5},{9,10},{10,9},{13,14},{14,13},{17,18},{18,... | collective-permute-start | bytes 3145736 | tf_op jit(solution)/shard_map/ppermute | solution.py:56
  230.9 7.7 %collective-permute-start.26 = (f32[512,512]{1,0:T(8,128)S(1)}, f32[512,512]{1,0:T(8,128)S(1)}, u32[]{:S(2)}, u32[]{:S(2)}) collective-permute-start(f32[512,512]{1,0:T(8,128)S(1)} %convolution_add_fusion.1), channel_id=1, source_target_pairs={{1,2},{2,1},{5,6},{6,5},{9,10},{10,9},{13,14},{14,13},{17,18},{18,... | collective-permute-start | bytes 3145736 | tf_op jit(solution)/shard_map/ppermute | solution.py:56
  232.1 8.2 %collective-permute-start.30 = (f32[512,512]{1,0:T(8,128)S(1)}, f32[512,512]{1,0:T(8,128)S(1)}, u32[]{:S(2)}, u32[]{:S(2)}) collective-permute-start(f32[512,512]{1,0:T(8,128)S(1)} %convolution_add_fusion), channel_id=1, source_target_pairs={{1,2},{2,1},{5,6},{6,5},{9,10},{10,9},{13,14},{14,13},{17,18},{18,... | collective-permute-start | bytes 3145736 | tf_op jit(solution)/shard_map/ppermute | solution.py:56
  233.3 116.9 %collective-permute-start.23 = (f32[256,512]{1,0:T(8,128)S(1)}, f32[256,512]{1,0:T(8,128)S(1)}, u32[]{:S(2)}, u32[]{:S(2)}) collective-permute-start(f32[256,512]{1,0:T(8,128)S(1)} %slice_add_fusion.2), channel_id=1, source_target_pairs={{1,0},{2,3},{5,4},{6,7},{9,8},{10,11},{13,12},{14,15},{17,16},{18,... | collective-permute-start | bytes 1572872 | tf_op jit(solution)/shard_map/ppermute | solution.py:58
  235.0 116.2 %collective-permute-start.19 = (f32[256,512]{1,0:T(8,128)S(1)}, f32[256,512]{1,0:T(8,128)S(1)}, u32[]{:S(2)}, u32[]{:S(2)}) collective-permute-start(f32[256,512]{1,0:T(8,128)S(1)} %slice_add_fusion.3), channel_id=1, source_target_pairs={{1,0},{2,3},{5,4},{6,7},{9,8},{10,11},{13,12},{14,15},{17,16},{18,... | collective-permute-start | bytes 1572872 | tf_op jit(solution)/shard_map/ppermute | solution.py:58
  236.8 101.9 %collective-permute-start.15 = (f32[256,512]{1,0:T(8,128)S(1)}, f32[256,512]{1,0:T(8,128)S(1)}, u32[]{:S(2)}, u32[]{:S(2)}) collective-permute-start(f32[256,512]{1,0:T(8,128)S(1)} %slice_add_fusion.4), channel_id=1, source_target_pairs={{1,0},{2,3},{5,4},{6,7},{9,8},{10,11},{13,12},{14,15},{17,16},{18,... | collective-permute-start | bytes 1572872 | tf_op jit(solution)/shard_map/ppermute | solution.py:58
  238.6 73.8 %collective-permute-start.7 = (f32[256,512]{1,0:T(8,128)S(1)}, f32[256,512]{1,0:T(8,128)S(1)}, u32[]{:S(2)}, u32[]{:S(2)}) collective-permute-start(f32[256,512]{1,0:T(8,128)S(1)} %slice_add_fusion.6), channel_id=1, source_target_pairs={{1,0},{2,3},{5,4},{6,7},{9,8},{10,11},{13,12},{14,15},{17,16},{18,... | collective-permute-start | bytes 1572872 | tf_op jit(solution)/shard_map/ppermute | solution.py:58
  240.3 96.6 %collective-permute-start.3 = (f32[256,512]{1,0:T(8,128)S(1)}, f32[256,512]{1,0:T(8,128)S(1)}, u32[]{:S(2)}, u32[]{:S(2)}) collective-permute-start(f32[256,512]{1,0:T(8,128)S(1)} %slice_add_fusion.7), channel_id=1, source_target_pairs={{1,0},{2,3},{5,4},{6,7},{9,8},{10,11},{13,12},{14,15},{17,16},{18,... | collective-permute-start | bytes 1572872 | tf_op jit(solution)/shard_map/ppermute | solution.py:58
  312.4 35.7 %collective-permute-start.11 = (f32[256,512]{1,0:T(8,128)S(1)}, f32[256,512]{1,0:T(8,128)S(1)}, u32[]{:S(2)}, u32[]{:S(2)}) collective-permute-start(f32[256,512]{1,0:T(8,128)S(1)} %slice_add_fusion.5), channel_id=1, source_target_pairs={{1,0},{2,3},{5,4},{6,7},{9,8},{10,11},{13,12},{14,15},{17,16},{18,... | collective-permute-start | bytes 1572872 | tf_op jit(solution)/shard_map/ppermute | solution.py:58
  336.9 22.5 %collective-permute-start.27 = (f32[256,512]{1,0:T(8,128)S(1)}, f32[256,512]{1,0:T(8,128)S(1)}, u32[]{:S(2)}, u32[]{:S(2)}) collective-permute-start(f32[256,512]{1,0:T(8,128)S(1)} %slice_add_fusion.1), channel_id=1, source_target_pairs={{1,0},{2,3},{5,4},{6,7},{9,8},{10,11},{13,12},{14,15},{17,16},{18,... | collective-permute-start | bytes 1572872 | tf_op jit(solution)/shard_map/ppermute | solution.py:58
  338.7 29.9 %collective-permute-start.31 = (f32[256,512]{1,0:T(8,128)S(1)}, f32[256,512]{1,0:T(8,128)S(1)}, u32[]{:S(2)}, u32[]{:S(2)}) collective-permute-start(f32[256,512]{1,0:T(8,128)S(1)} %slice_add_fusion), channel_id=1, source_target_pairs={{1,0},{2,3},{5,4},{6,7},{9,8},{10,11},{13,12},{14,15},{17,16},{18,... | collective-permute-start | bytes 1572872 | tf_op jit(solution)/shard_map/ppermute | solution.py:58
  348.1 22.9 %collective-permute-start.4 = (f32[128,512]{1,0:T(8,128)S(1)}, f32[128,512]{1,0:T(8,128)S(1)}, u32[]{:S(2)}, u32[]{:S(2)}) collective-permute-start(f32[128,512]{1,0:T(8,128)S(1)} %dynamic-slice_bitcast_fusion.7), channel_id=1, source_target_pairs={{0,8},{8,0},{1,9},{9,1},{2,10},{10,2},{3,11},{11,3},{4,12},{12,4},... | collective-permute-start | bytes 786440 | tf_op jit(solution)/shard_map/ppermute | solution.py:66
  350.2 21.6 %collective-permute-start.8 = (f32[128,512]{1,0:T(8,128)S(1)}, f32[128,512]{1,0:T(8,128)S(1)}, u32[]{:S(2)}, u32[]{:S(2)}) collective-permute-start(f32[128,512]{1,0:T(8,128)S(1)} %dynamic-slice_bitcast_fusion.6), channel_id=1, source_target_pairs={{0,8},{8,0},{1,9},{9,1},{2,10},{10,2},{3,11},{11,3},{4,12},{12,4},... | collective-permute-start | bytes 786440 | tf_op jit(solution)/shard_map/ppermute | solution.py:66
  351.3 22.1 %collective-permute-start.12 = (f32[128,512]{1,0:T(8,128)S(1)}, f32[128,512]{1,0:T(8,128)S(1)}, u32[]{:S(2)}, u32[]{:S(2)}) collective-permute-start(f32[128,512]{1,0:T(8,128)S(1)} %dynamic-slice_bitcast_fusion.5), channel_id=1, source_target_pairs={{0,8},{8,0},{1,9},{9,1},{2,10},{10,2},{3,11},{11,3},{4,12},{12,4},... | collective-permute-start | bytes 786440 | tf_op jit(solution)/shard_map/ppermute | solution.py:66
  359.4 14.7 %collective-permute-start.16 = (f32[128,512]{1,0:T(8,128)S(1)}, f32[128,512]{1,0:T(8,128)S(1)}, u32[]{:S(2)}, u32[]{:S(2)}) collective-permute-start(f32[128,512]{1,0:T(8,128)S(1)} %dynamic-slice_bitcast_fusion.4), channel_id=1, source_target_pairs={{0,8},{8,0},{1,9},{9,1},{2,10},{10,2},{3,11},{11,3},{4,12},{12,4},... | collective-permute-start | bytes 786440 | tf_op jit(solution)/shard_map/ppermute | solution.py:66
  368.6 9.2 %collective-permute-start.20 = (f32[128,512]{1,0:T(8,128)S(1)}, f32[128,512]{1,0:T(8,128)S(1)}, u32[]{:S(2)}, u32[]{:S(2)}) collective-permute-start(f32[128,512]{1,0:T(8,128)S(1)} %dynamic-slice_bitcast_fusion.3), channel_id=1, source_target_pairs={{0,8},{8,0},{1,9},{9,1},{2,10},{10,2},{3,11},{11,3},{4,12},{12,4},... | collective-permute-start | bytes 786440 | tf_op jit(solution)/shard_map/ppermute | solution.py:66
  371.1 12.3 %collective-permute-start.24 = (f32[128,512]{1,0:T(8,128)S(1)}, f32[128,512]{1,0:T(8,128)S(1)}, u32[]{:S(2)}, u32[]{:S(2)}) collective-permute-start(f32[128,512]{1,0:T(8,128)S(1)} %dynamic-slice_bitcast_fusion.2), channel_id=1, source_target_pairs={{0,8},{8,0},{1,9},{9,1},{2,10},{10,2},{3,11},{11,3},{4,12},{12,4},... | collective-permute-start | bytes 786440 | tf_op jit(solution)/shard_map/ppermute | solution.py:66
  371.7 17.2 %collective-permute-start.28 = (f32[128,512]{1,0:T(8,128)S(1)}, f32[128,512]{1,0:T(8,128)S(1)}, u32[]{:S(2)}, u32[]{:S(2)}) collective-permute-start(f32[128,512]{1,0:T(8,128)S(1)} %dynamic-slice_bitcast_fusion.1), channel_id=1, source_target_pairs={{0,8},{8,0},{1,9},{9,1},{2,10},{10,2},{3,11},{11,3},{4,12},{12,4},... | collective-permute-start | bytes 786440 | tf_op jit(solution)/shard_map/ppermute | solution.py:66
  373.4 18.4 %collective-permute-start.32 = (f32[128,512]{1,0:T(8,128)S(1)}, f32[128,512]{1,0:T(8,128)S(1)}, u32[]{:S(2)}, u32[]{:S(2)}) collective-permute-start(f32[128,512]{1,0:T(8,128)S(1)} %dynamic-slice_bitcast_fusion), channel_id=1, source_target_pairs={{0,8},{8,0},{1,9},{9,1},{2,10},{10,2},{3,11},{11,3},{4,12},{12,4},... | collective-permute-start | bytes 786440 | tf_op jit(solution)/shard_map/ppermute | solution.py:66
  389.0 2.7 copy-start
Sparse Core Ops, SparseCore 0:
  8.9 11.7 all-gather.4
  26.0 10.0 all-gather.8
  37.7 34.2 all-gather.6
  73.4 33.0 all-gather.10
where the time goes:
time: 400 us; the launch traced here: 399 us
  waiting for transfers between devices  294 us (74%)
  starting transfers between devices  47.8 us (12%)
  matrix products  29.8 us (7%)
  between operations  14 us (4%)
  local copies, waits for them, and re-layouts  13.4 us (3%)
    ppermute x8, waiting for transfers between devices, on_device(): from_inner = lax.ppermute(to_outer, 'layer', outward)  111 us
    ppermute x8, waiting for transfers between devices, on_device(): theirs = lax.ppermute(mine, 'layer', inward)  90.4 us
    all_gather x2, waiting for transfers between devices, full_dosages(): return lax.all_gather(samples, 'row', axis=1, tiled=True)  53.1 us
    dot_general x40, matrix products, contract(): lax.dot_general(left_rows, right_rows, (((0,), (0,)), ((), ())), preferre...  29.8 us
    ppermute x8, waiting for transfers between devices, on_device(): piece = lax.ppermute(piece, 'row', pairs)  17.4 us
    ppermute x8, starting transfers between devices, on_device(): theirs = lax.ppermute(mine, 'layer', inward)  17.1 us
    ppermute x1, waiting for transfers between devices, on_device(): dosages_in = lax.ppermute(dosages, 'layer', inward)  11.4 us
    ppermute x8, starting transfers between devices, on_device(): from_inner = lax.ppermute(to_outer, 'layer', outward)  10.3 us
  transfers between devices with their start and end apart: 37, of which 18 were waited for; matrix products, arithmetic and copies ran while one was open for 10% of the time, Pallas kernels for 0%

commit v1 on v0

--- a/solution.py
+++ b/solution.py
@@ -3,6 +3,7 @@
 import jax.numpy as jnp
 from jax import lax
 from jax.sharding import PartitionSpec as P
+from jax.lax import all_to_all, axis_size
 
 
 def contract(left_rows, right_rows):
@@ -12,7 +13,9 @@
 
 
 def full_dosages(local):
-    samples = lax.all_gather(local, "col", axis=0, tiled=True)
+    samples = jnp.concatenate(
+        all_to_all(jnp.stack(axis_size("col") * [local], axis=0), "col", 0, 0), axis=0
+    )
     return lax.all_gather(samples, "row", axis=1, tiled=True)
 
 

time: 400 us -> 426 us (1.065)
  waiting for transfers between devices: 294 us -> 306 us
  blocking collectives: 0 us -> 9.15 us
    all_gather x2, waiting for transfers between devices: 53.1 us -> 30.1 us  [full_dosages(): return lax.all_gather(samples, 'row', axis=1, tiled=True)]
    ppermute x8, waiting for transfers between devices: 90.4 us -> 110 us  [on_device(): theirs = lax.ppermute(mine, 'layer', inward)]
    ppermute x8, waiting for transfers between devices: 111 us -> 129 us  [on_device(): from_inner = lax.ppermute(to_outer, 'layer', outward)]
    all_gather x2 -> x0, waiting for transfers between devices: 9.45 us -> none  [full_dosages(): samples = lax.all_gather(local, 'col', axis=0, tiled=True)]
    all_to_all x0 -> x2, blocking collectives: none -> 9.15 us  [full_dosages(): all_to_all(jnp.stack(axis_size('col') * [local], axis=0), 'col', 0, 0)]
    ppermute x8, waiting for transfers between devices: 17.4 us -> 24.9 us  [on_device(): piece = lax.ppermute(piece, 'row', pairs)]
  transfers between devices with their start and end apart: 37 -> 35, of which waited for: 18 -> 19; matrix products, arithmetic and copies ran while one was open for 10% -> 10% of each run, Pallas kernels for 0% -> 0%
where the time goes in v1:
time: 426 us; the launch traced here: 425 us
  waiting for transfers between devices  306 us (72%)
  starting transfers between devices  51.7 us (12%)
  matrix products  29.8 us (7%)
  between operations  14.3 us (3%)
  local copies, waits for them, and re-layouts  13.2 us (3%)
  blocking collectives  9.15 us (2%)
    ppermute x8, waiting for transfers between devices, on_device(): from_inner = lax.ppermute(to_outer, 'layer', outward)  129 us
    ppermute x8, waiting for transfers between devices, on_device(): theirs = lax.ppermute(mine, 'layer', inward)  110 us
    all_gather x2, waiting for transfers between devices, full_dosages(): return lax.all_gather(samples, 'row', axis=1, tiled=True)  30.1 us
    dot_general x40, matrix products, contract(): lax.dot_general(left_rows, right_rows, (((0,), (0,)), ((), ())), preferre...  29.8 us
    ppermute x8, waiting for transfers between devices, on_device(): piece = lax.ppermute(piece, 'row', pairs)  24.9 us
    ppermute x8, starting transfers between devices, on_device(): theirs = lax.ppermute(mine, 'layer', inward)  21 us
    ppermute x1, waiting for transfers between devices, on_device(): dosages_in = lax.ppermute(dosages, 'layer', inward)  11.4 us
    ppermute x8, starting transfers between devices, on_device(): from_inner = lax.ppermute(to_outer, 'layer', outward)  10.3 us
  transfers between devices with their start and end apart: 35, of which 19 were waited for; matrix products, arithmetic and copies ran while one was open for 10% of the time, Pallas kernels for 0%

profile of v1, /device:TPU:0, one launch (start us, length us, event | category | flops | bytes accessed | tf_op | source)
XLA Modules:
  0.0 425.1 jit_solution(17946598774824707199)
XLA Ops:
  6.5 1.4 pad_maximum_fusion
  7.9 4.6 %all_to_all.10 = bf16[2,512,512]{2,1,0:T(8,128)(2,1)S(1)} all-to-all(bf16[2,512,512]{2,1,0:T(8,128)(2,1)S(1)} %pad_maximum_fusion), channel_id=1, replica_groups=mesh['parts'=2,'row'=2,'col'=2,'layer'=4] {'col'}, dimensions={0} | all-to-all | bytes 2097152 | tf_op jit(solution)/shard_map/all_to_all | solution.py:17
  12.5 1.3 copy.5
  13.9 5.0 %collective-permute-start = (bf16[512,512]{1,0:T(8,128)(2,1)S(1)}, bf16[512,512]{1,0:T(8,128)(2,1)S(1)}, u32[]{:S(2)}, u32[]{:S(2)}) collective-permute-start(bf16[512,512]{1,0:T(8,128)(2,1)S(1)} %copy-done.4), channel_id=1, source_target_pairs={{0,1},{3,2},{4,5},{7,6},{8,9},{11,10},{12,13},{15,14},{16,17},{19,... | collective-permute-start | bytes 1572872 | tf_op jit(solution)/shard_map/ppermute | solution.py:39
  18.9 11.4 %collective-permute-done = bf16[512,512]{1,0:T(8,128)(2,1)S(1)} collective-permute-done((bf16[512,512]{1,0:T(8,128)(2,1)S(1)}, bf16[512,512]{1,0:T(8,128)(2,1)S(1)}, u32[]{:S(2)}, u32[]{:S(2)}) %collective-permute-start) | collective-permute-done | bytes 524320 | tf_op jit(solution)/shard_map/ppermute | solution.py:39
  30.4 4.6 %all_to_all.11 = bf16[2,512,512]{2,1,0:T(8,128)(2,1)S(1)} all-to-all(bf16[2,512,512]{2,1,0:T(8,128)(2,1)S(1)} %pad_maximum_fusion.1), channel_id=1, replica_groups=mesh['parts'=2,'row'=2,'col'=2,'layer'=4] {'col'}, dimensions={0} | all-to-all | bytes 2097152 | tf_op jit(solution)/shard_map/all_to_all | solution.py:17
  35.0 1.3 copy.6
  36.3 6.3 %fusion.88 = (bf16[1024,512]{1,0:T(8,128)(2,1)}, bf16[1024,512]{1,0:T(8,128)(2,1)}, bf16[1024,512]{1,0:T(8,128)(2,1)}, bf16[1024,512]{1,0:T(8,128)(2,1)}, bf16[1...) fusion(bf16[1024,4096]{1,0:T(8,128)(2,1)} %param.3), kind=kLoop, calls=%fused_computation.131 | loop fusion | bytes 16777216 | tf_op jit(solution)/shard_map/slice | solution.py:56
  42.6 4.5 %collective-permute-start.29 = (bf16[1024,512]{1,0:T(8,128)(2,1)}, bf16[1024,512]{1,0:T(8,128)(2,1)S(1)}, u32[]{:S(2)}, u32[]{:S(2)}) collective-permute-start(bf16[1024,512]{1,0:T(8,128)(2,1)} %get-tuple-element.5), channel_id=1, source_target_pairs={{0,1},{3,2},{4,5},{7,6},{8,9},{11,10},{12,13},{15,14},{16,17},{19,... | collective-permute-start | bytes 3145736 | tf_op jit(solution)/shard_map/ppermute | solution.py:57
  47.1 1.4 collective-permute-start.25
  48.4 2.3 collective-permute-start.21
  50.7 1.3 collective-permute-start.17
  52.1 2.3 collective-permute-start.13
  54.4 30.1 %all-gather.5.cloned.1.call-done = bf16[1024,1024]{0,1:T(8,128)(2,1)} async-done(((bf16[1024,512]{0,1:T(8,128)(2,1)}), bf16[1024,1024]{0,1:T(8,128)(2,1)}) %all-gather.5.cloned.1.call-update) | async-done | bytes 2097168 | tf_op jit(solution)/shard_map/all_gather | solution.py:19
  84.5 2.5 constant_dynamic-slice_fusion.5
  87.0 2.1 fusion.26
  89.1 1.9 fusion.34
  94.3 3.5 collective-permute-start.9
  98.6 1.4 collective-permute-start.5
  100.6 15.1 %collective-permute-done.21 = bf16[1024,512]{1,0:T(8,128)(2,1)} collective-permute-done((bf16[1024,512]{1,0:T(8,128)(2,1)}, bf16[1024,512]{1,0:T(8,128)(2,1)}, u32[]{:S(2)}, u32[]{:S(2)}) %collective-permute-start.21) | collective-permute-done | bytes 1048608 | tf_op jit(solution)/shard_map/ppermute | solution.py:57
  115.8 4.4 %collective-permute-start.1 = (bf16[1024,512]{1,0:T(8,128)(2,1)S(1)}, bf16[1024,512]{1,0:T(8,128)(2,1)S(1)}, u32[]{:S(2)}, u32[]{:S(2)}) collective-permute-start(bf16[1024,512]{1,0:T(8,128)(2,1)S(1)} %copy-done.1), channel_id=1, source_target_pairs={{0,1},{3,2},{4,5},{7,6},{8,9},{11,10},{12,13},{15,14},{16,17},{19,... | collective-permute-start | bytes 3145736 | tf_op jit(solution)/shard_map/ppermute | solution.py:57
  120.2 1.9 convolution_add_fusion.2
  122.2 16.1 %collective-permute-done.17 = bf16[1024,512]{1,0:T(8,128)(2,1)S(1)} collective-permute-done((bf16[1024,512]{1,0:T(8,128)(2,1)}, bf16[1024,512]{1,0:T(8,128)(2,1)S(1)}, u32[]{:S(2)}, u32[]{:S(2)}) %collective-permute-start.17) | collective-permute-done | bytes 1048608 | tf_op jit(solution)/shard_map/ppermute | solution.py:57
  142.6 18.2 %collective-permute-done.13 = bf16[1024,512]{1,0:T(8,128)(2,1)} collective-permute-done((bf16[1024,512]{1,0:T(8,128)(2,1)}, bf16[1024,512]{1,0:T(8,128)(2,1)}, u32[]{:S(2)}, u32[]{:S(2)}) %collective-permute-start.13) | collective-permute-done | bytes 1048608 | tf_op jit(solution)/shard_map/ppermute | solution.py:57
  161.4 1.9 convolution_add_fusion.4
  163.4 19.7 %collective-permute-done.9 = bf16[1024,512]{1,0:T(8,128)(2,1)S(1)} collective-permute-done((bf16[1024,512]{1,0:T(8,128)(2,1)S(1)}, bf16[1024,512]{1,0:T(8,128)(2,1)S(1)}, u32[]{:S(2)}, u32[]{:S(2)}) %collective-permute-start.9) | collective-permute-done | bytes 1048608 | tf_op jit(solution)/shard_map/ppermute | solution.py:57
  184.7 20.9 %collective-permute-done.5 = bf16[1024,512]{1,0:T(8,128)(2,1)S(1)} collective-permute-done((bf16[1024,512]{1,0:T(8,128)(2,1)S(1)}, bf16[1024,512]{1,0:T(8,128)(2,1)S(1)}, u32[]{:S(2)}, u32[]{:S(2)}) %collective-permute-start.5) | collective-permute-done | bytes 1048608 | tf_op jit(solution)/shard_map/ppermute | solution.py:57
  207.0 20.2 %collective-permute-done.1 = bf16[1024,512]{1,0:T(8,128)(2,1)S(1)} collective-permute-done((bf16[1024,512]{1,0:T(8,128)(2,1)S(1)}, bf16[1024,512]{1,0:T(8,128)(2,1)S(1)}, u32[]{:S(2)}, u32[]{:S(2)}) %collective-permute-start.1) | collective-permute-done | bytes 1048608 | tf_op jit(solution)/shard_map/ppermute | solution.py:57
  234.0 1.3 collective-permute-start.31
  235.8 1.3 collective-permute-start.27
  237.5 1.3 collective-permute-start.23
  242.8 98.1 %collective-permute-done.7 = f32[256,512]{1,0:T(8,128)S(1)} collective-permute-done((f32[256,512]{1,0:T(8,128)S(1)}, f32[256,512]{1,0:T(8,128)S(1)}, u32[]{:S(2)}, u32[]{:S(2)}) %collective-permute-start.7) | collective-permute-done | bytes 524320 | tf_op jit(solution)/shard_map/ppermute | solution.py:61
  342.7 9.5 %collective-permute-done.3 = f32[256,512]{1,0:T(8,128)S(1)} collective-permute-done((f32[256,512]{1,0:T(8,128)S(1)}, f32[256,512]{1,0:T(8,128)S(1)}, u32[]{:S(2)}, u32[]{:S(2)}) %collective-permute-start.3) | collective-permute-done | bytes 524320 | tf_op jit(solution)/shard_map/ppermute | solution.py:61
  354.0 9.4 %collective-permute-done.15 = f32[256,512]{1,0:T(8,128)S(1)} collective-permute-done((f32[256,512]{1,0:T(8,128)S(1)}, f32[256,512]{1,0:T(8,128)S(1)}, u32[]{:S(2)}, u32[]{:S(2)}) %collective-permute-start.15) | collective-permute-done | bytes 524320 | tf_op jit(solution)/shard_map/ppermute | solution.py:61
  364.7 1.7 fusion.17
  366.4 8.2 %collective-permute-done.11 = f32[256,512]{1,0:T(8,128)S(1)} collective-permute-done((f32[256,512]{1,0:T(8,128)S(1)}, f32[256,512]{1,0:T(8,128)S(1)}, u32[]{:S(2)}, u32[]{:S(2)}) %collective-permute-start.11) | collective-permute-done | bytes 524320 | tf_op jit(solution)/shard_map/ppermute | solution.py:61
  374.6 1.5 collective-permute-start.4
  377.3 1.7 fusion.13
  379.0 3.8 collective-permute-done.19
  382.8 1.5 collective-permute-start.12
  386.0 1.6 collective-permute-start.20
  389.2 1.6 collective-permute-start.28
  392.0 1.5 collective-permute-start.32
  393.5 4.1 collective-permute-done.16
  397.7 5.6 %collective-permute-done.20 = f32[128,512]{1,0:T(8,128)S(1)} collective-permute-done((f32[128,512]{1,0:T(8,128)S(1)}, f32[128,512]{1,0:T(8,128)S(1)}, u32[]{:S(2)}, u32[]{:S(2)}) %collective-permute-start.20) | collective-permute-done | bytes 262176 | tf_op jit(solution)/shard_map/ppermute | solution.py:69
  403.3 5.6 %collective-permute-done.24 = f32[128,512]{1,0:T(8,128)S(1)} collective-permute-done((f32[128,512]{1,0:T(8,128)S(1)}, f32[128,512]{1,0:T(8,128)S(1)}, u32[]{:S(2)}, u32[]{:S(2)}) %collective-permute-start.24) | collective-permute-done | bytes 262176 | tf_op jit(solution)/shard_map/ppermute | solution.py:69
  408.9 5.6 %collective-permute-done.28 = f32[128,512]{1,0:T(8,128)S(1)} collective-permute-done((f32[128,512]{1,0:T(8,128)S(1)}, f32[128,512]{1,0:T(8,128)S(1)}, u32[]{:S(2)}, u32[]{:S(2)}) %collective-permute-start.28) | collective-permute-done | bytes 262176 | tf_op jit(solution)/shard_map/ppermute | solution.py:69
  414.5 3.0 collective-permute-done.32
  (112 shorter events, 35.7 us)
Async XLA Ops:
  6.5 7.3 %copy-start.4 = (bf16[512,512]{1,0:T(8,128)(2,1)S(1)}, bf16[512,512]{1,0:T(8,128)(2,1)}, u32[]{:S(2)}) copy-start(bf16[512,512]{1,0:T(8,128)(2,1)} %param.2) | copy-start | bytes 1572868
  6.5 47.8 %all-gather.3.cloned.1.call-start = ((), (), s32[]{:S(2)}) async-start(), calls=%async_computation.2 | async-start | bytes 3145728 | tf_op jit(solution)/shard_map/all_gather | solution.py:19
  13.8 70.6 %all-gather.5.cloned.1.call-start = ((), (), s32[]{:S(2)}) async-start(), calls=%async_computation.3 | async-start | bytes 3145728 | tf_op jit(solution)/shard_map/all_gather | solution.py:19
  13.9 16.4 %collective-permute-start = (bf16[512,512]{1,0:T(8,128)(2,1)S(1)}, bf16[512,512]{1,0:T(8,128)(2,1)S(1)}, u32[]{:S(2)}, u32[]{:S(2)}) collective-permute-start(bf16[512,512]{1,0:T(8,128)(2,1)S(1)} %copy-done.4), channel_id=1, source_target_pairs={{0,1},{3,2},{4,5},{7,6},{8,9},{11,10},{12,13},{15,14},{16,17},{19,... | collective-permute-start | bytes 1572872 | tf_op jit(solution)/shard_map/ppermute | solution.py:39
  42.6 51.7 %collective-permute-start.29 = (bf16[1024,512]{1,0:T(8,128)(2,1)}, bf16[1024,512]{1,0:T(8,128)(2,1)S(1)}, u32[]{:S(2)}, u32[]{:S(2)}) collective-permute-start(bf16[1024,512]{1,0:T(8,128)(2,1)} %get-tuple-element.5), channel_id=1, source_target_pairs={{0,1},{3,2},{4,5},{7,6},{8,9},{11,10},{12,13},{15,14},{16,17},{19,... | collective-permute-start | bytes 3145736 | tf_op jit(solution)/shard_map/ppermute | solution.py:57
  47.1 51.5 %collective-permute-start.25 = (bf16[1024,512]{1,0:T(8,128)(2,1)}, bf16[1024,512]{1,0:T(8,128)(2,1)S(1)}, u32[]{:S(2)}, u32[]{:S(2)}) collective-permute-start(bf16[1024,512]{1,0:T(8,128)(2,1)} %get-tuple-element.12), channel_id=1, source_target_pairs={{0,1},{3,2},{4,5},{7,6},{8,9},{11,10},{12,13},{15,14},{16,17},{19,... | collective-permute-start | bytes 3145736 | tf_op jit(solution)/shard_map/ppermute | solution.py:57
  48.4 67.4 %collective-permute-start.21 = (bf16[1024,512]{1,0:T(8,128)(2,1)}, bf16[1024,512]{1,0:T(8,128)(2,1)}, u32[]{:S(2)}, u32[]{:S(2)}) collective-permute-start(bf16[1024,512]{1,0:T(8,128)(2,1)} %get-tuple-element.6), channel_id=1, source_target_pairs={{0,1},{3,2},{4,5},{7,6},{8,9},{11,10},{12,13},{15,14},{16,17},{19,... | collective-permute-start | bytes 3145736 | tf_op jit(solution)/shard_map/ppermute | solution.py:57
  50.7 87.5 %collective-permute-start.17 = (bf16[1024,512]{1,0:T(8,128)(2,1)}, bf16[1024,512]{1,0:T(8,128)(2,1)S(1)}, u32[]{:S(2)}, u32[]{:S(2)}) collective-permute-start(bf16[1024,512]{1,0:T(8,128)(2,1)} %get-tuple-element.7), channel_id=1, source_target_pairs={{0,1},{3,2},{4,5},{7,6},{8,9},{11,10},{12,13},{15,14},{16,17},{19,... | collective-permute-start | bytes 3145736 | tf_op jit(solution)/shard_map/ppermute | solution.py:57
  52.1 108.6 %collective-permute-start.13 = (bf16[1024,512]{1,0:T(8,128)(2,1)}, bf16[1024,512]{1,0:T(8,128)(2,1)}, u32[]{:S(2)}, u32[]{:S(2)}) collective-permute-start(bf16[1024,512]{1,0:T(8,128)(2,1)} %get-tuple-element.8), channel_id=1, source_target_pairs={{0,1},{3,2},{4,5},{7,6},{8,9},{11,10},{12,13},{15,14},{16,17},{19,... | collective-permute-start | bytes 3145736 | tf_op jit(solution)/shard_map/ppermute | solution.py:57
  84.5 6.6 %slice-start = ((s8[8388608]{0:T(1024)(128)(4,1)}), s8[4194304]{0:T(1024)(128)(4,1)S(1)}, s32[]{:S(2)}) async-start(s8[8388608]{0:T(1024)(128)(4,1)} %bitcast.109), calls=%async_computation.4 | async-start | bytes 8388608
  87.0 4.1 slice-start.1
  92.7 1.6 copy-start.3
  93.9 4.7 %copy-start.2 = (bf16[1024,512]{1,0:T(8,128)(2,1)S(1)}, bf16[1024,512]{1,0:T(8,128)(2,1)}, u32[]{:S(2)}) copy-start(bf16[1024,512]{1,0:T(8,128)(2,1)} %get-tuple-element.10) | copy-start | bytes 3145732
  94.3 88.7 %collective-permute-start.9 = (bf16[1024,512]{1,0:T(8,128)(2,1)S(1)}, bf16[1024,512]{1,0:T(8,128)(2,1)S(1)}, u32[]{:S(2)}, u32[]{:S(2)}) collective-permute-start(bf16[1024,512]{1,0:T(8,128)(2,1)S(1)} %copy-done.3), channel_id=1, source_target_pairs={{0,1},{3,2},{4,5},{7,6},{8,9},{11,10},{12,13},{15,14},{16,17},{19,... | collective-permute-start | bytes 3145736 | tf_op jit(solution)/shard_map/ppermute | solution.py:57
  97.8 18.0 %copy-start.1 = (bf16[1024,512]{1,0:T(8,128)(2,1)S(1)}, bf16[1024,512]{1,0:T(8,128)(2,1)}, u32[]{:S(2)}) copy-start(bf16[1024,512]{1,0:T(8,128)(2,1)} %get-tuple-element.11) | copy-start | bytes 3145732
  98.6 107.0 %collective-permute-start.5 = (bf16[1024,512]{1,0:T(8,128)(2,1)S(1)}, bf16[1024,512]{1,0:T(8,128)(2,1)S(1)}, u32[]{:S(2)}, u32[]{:S(2)}) collective-permute-start(bf16[1024,512]{1,0:T(8,128)(2,1)S(1)} %copy-done.2), channel_id=1, source_target_pairs={{0,1},{3,2},{4,5},{7,6},{8,9},{11,10},{12,13},{15,14},{16,17},{19,... | collective-permute-start | bytes 3145736 | tf_op jit(solution)/shard_map/ppermute | solution.py:57
  115.8 111.4 %collective-permute-start.1 = (bf16[1024,512]{1,0:T(8,128)(2,1)S(1)}, bf16[1024,512]{1,0:T(8,128)(2,1)S(1)}, u32[]{:S(2)}, u32[]{:S(2)}) collective-permute-start(bf16[1024,512]{1,0:T(8,128)(2,1)S(1)} %copy-done.1), channel_id=1, source_target_pairs={{0,1},{3,2},{4,5},{7,6},{8,9},{11,10},{12,13},{15,14},{16,17},{19,... | collective-permute-start | bytes 3145736 | tf_op jit(solution)/shard_map/ppermute | solution.py:57
  141.8 88.6 %collective-permute-start.30 = (f32[512,512]{1,0:T(8,128)S(1)}, f32[512,512]{1,0:T(8,128)S(1)}, u32[]{:S(2)}, u32[]{:S(2)}) collective-permute-start(f32[512,512]{1,0:T(8,128)S(1)} %convolution_add_fusion), channel_id=1, source_target_pairs={{1,2},{2,1},{5,6},{6,5},{9,10},{10,9},{13,14},{14,13},{17,18},{18,... | collective-permute-start | bytes 3145736 | tf_op jit(solution)/shard_map/ppermute | solution.py:59
  160.7 70.9 %collective-permute-start.26 = (f32[512,512]{1,0:T(8,128)S(1)}, f32[512,512]{1,0:T(8,128)S(1)}, u32[]{:S(2)}, u32[]{:S(2)}) collective-permute-start(f32[512,512]{1,0:T(8,128)S(1)} %convolution_add_fusion.1), channel_id=1, source_target_pairs={{1,2},{2,1},{5,6},{6,5},{9,10},{10,9},{13,14},{14,13},{17,18},{18,... | collective-permute-start | bytes 3145736 | tf_op jit(solution)/shard_map/ppermute | solution.py:59
  183.1 49.7 %collective-permute-start.22 = (f32[512,512]{1,0:T(8,128)S(1)}, f32[512,512]{1,0:T(8,128)S(1)}, u32[]{:S(2)}, u32[]{:S(2)}) collective-permute-start(f32[512,512]{1,0:T(8,128)S(1)} %convolution_add_fusion.2), channel_id=1, source_target_pairs={{1,2},{2,1},{5,6},{6,5},{9,10},{10,9},{13,14},{14,13},{17,18},{18,... | collective-permute-start | bytes 3145736 | tf_op jit(solution)/shard_map/ppermute | solution.py:59
  205.6 28.5 %collective-permute-start.18 = (f32[512,512]{1,0:T(8,128)S(1)}, f32[512,512]{1,0:T(8,128)S(1)}, u32[]{:S(2)}, u32[]{:S(2)}) collective-permute-start(f32[512,512]{1,0:T(8,128)S(1)} %convolution_add_fusion.3), channel_id=1, source_target_pairs={{1,2},{2,1},{5,6},{6,5},{9,10},{10,9},{13,14},{14,13},{17,18},{18,... | collective-permute-start | bytes 3145736 | tf_op jit(solution)/shard_map/ppermute | solution.py:59
  227.2 8.6 %collective-permute-start.14 = (f32[512,512]{1,0:T(8,128)S(1)}, f32[512,512]{1,0:T(8,128)S(1)}, u32[]{:S(2)}, u32[]{:S(2)}) collective-permute-start(f32[512,512]{1,0:T(8,128)S(1)} %convolution_add_fusion.4), channel_id=1, source_target_pairs={{1,2},{2,1},{5,6},{6,5},{9,10},{10,9},{13,14},{14,13},{17,18},{18,... | collective-permute-start | bytes 3145736 | tf_op jit(solution)/shard_map/ppermute | solution.py:59
  230.4 10.6 %collective-permute-start.10 = (f32[512,512]{1,0:T(8,128)S(1)}, f32[512,512]{1,0:T(8,128)S(1)}, u32[]{:S(2)}, u32[]{:S(2)}) collective-permute-start(f32[512,512]{1,0:T(8,128)S(1)} %convolution_add_fusion.5), channel_id=1, source_target_pairs={{1,2},{2,1},{5,6},{6,5},{9,10},{10,9},{13,14},{14,13},{17,18},{18,... | collective-permute-start | bytes 3145736 | tf_op jit(solution)/shard_map/ppermute | solution.py:59
  231.6 5.9 %collective-permute-start.6 = (f32[512,512]{1,0:T(8,128)S(1)}, f32[512,512]{1,0:T(8,128)S(1)}, u32[]{:S(2)}, u32[]{:S(2)}) collective-permute-start(f32[512,512]{1,0:T(8,128)S(1)} %convolution_add_fusion.6), channel_id=1, source_target_pairs={{1,2},{2,1},{5,6},{6,5},{9,10},{10,9},{13,14},{14,13},{17,18},{18,... | collective-permute-start | bytes 3145736 | tf_op jit(solution)/shard_map/ppermute | solution.py:59
  232.8 6.5 %collective-permute-start.2 = (f32[512,512]{1,0:T(8,128)S(1)}, f32[512,512]{1,0:T(8,128)S(1)}, u32[]{:S(2)}, u32[]{:S(2)}) collective-permute-start(f32[512,512]{1,0:T(8,128)S(1)} %convolution_add_fusion.7), channel_id=1, source_target_pairs={{1,2},{2,1},{5,6},{6,5},{9,10},{10,9},{13,14},{14,13},{17,18},{18,... | collective-permute-start | bytes 3145736 | tf_op jit(solution)/shard_map/ppermute | solution.py:59
  234.0 150.8 %collective-permute-start.31 = (f32[256,512]{1,0:T(8,128)S(1)}, f32[256,512]{1,0:T(8,128)S(1)}, u32[]{:S(2)}, u32[]{:S(2)}) collective-permute-start(f32[256,512]{1,0:T(8,128)S(1)} %slice_add_fusion), channel_id=1, source_target_pairs={{1,0},{2,3},{5,4},{6,7},{9,8},{10,11},{13,12},{14,15},{17,16},{18,... | collective-permute-start | bytes 1572872 | tf_op jit(solution)/shard_map/ppermute | solution.py:61
  235.8 150.2 %collective-permute-start.27 = (f32[256,512]{1,0:T(8,128)S(1)}, f32[256,512]{1,0:T(8,128)S(1)}, u32[]{:S(2)}, u32[]{:S(2)}) collective-permute-start(f32[256,512]{1,0:T(8,128)S(1)} %slice_add_fusion.1), channel_id=1, source_target_pairs={{1,0},{2,3},{5,4},{6,7},{9,8},{10,11},{13,12},{14,15},{17,16},{18,... | collective-permute-start | bytes 1572872 | tf_op jit(solution)/shard_map/ppermute | solution.py:61
  237.5 139.2 %collective-permute-start.23 = (f32[256,512]{1,0:T(8,128)S(1)}, f32[256,512]{1,0:T(8,128)S(1)}, u32[]{:S(2)}, u32[]{:S(2)}) collective-permute-start(f32[256,512]{1,0:T(8,128)S(1)} %slice_add_fusion.2), channel_id=1, source_target_pairs={{1,0},{2,3},{5,4},{6,7},{9,8},{10,11},{13,12},{14,15},{17,16},{18,... | collective-permute-start | bytes 1572872 | tf_op jit(solution)/shard_map/ppermute | solution.py:61
  239.3 101.6 %collective-permute-start.7 = (f32[256,512]{1,0:T(8,128)S(1)}, f32[256,512]{1,0:T(8,128)S(1)}, u32[]{:S(2)}, u32[]{:S(2)}) collective-permute-start(f32[256,512]{1,0:T(8,128)S(1)} %slice_add_fusion.6), channel_id=1, source_target_pairs={{1,0},{2,3},{5,4},{6,7},{9,8},{10,11},{13,12},{14,15},{17,16},{18,... | collective-permute-start | bytes 1572872 | tf_op jit(solution)/shard_map/ppermute | solution.py:61
  241.1 111.1 %collective-permute-start.3 = (f32[256,512]{1,0:T(8,128)S(1)}, f32[256,512]{1,0:T(8,128)S(1)}, u32[]{:S(2)}, u32[]{:S(2)}) collective-permute-start(f32[256,512]{1,0:T(8,128)S(1)} %slice_add_fusion.7), channel_id=1, source_target_pairs={{1,0},{2,3},{5,4},{6,7},{9,8},{10,11},{13,12},{14,15},{17,16},{18,... | collective-permute-start | bytes 1572872 | tf_op jit(solution)/shard_map/ppermute | solution.py:61
  340.9 22.5 %collective-permute-start.15 = (f32[256,512]{1,0:T(8,128)S(1)}, f32[256,512]{1,0:T(8,128)S(1)}, u32[]{:S(2)}, u32[]{:S(2)}) collective-permute-start(f32[256,512]{1,0:T(8,128)S(1)} %slice_add_fusion.4), channel_id=1, source_target_pairs={{1,0},{2,3},{5,4},{6,7},{9,8},{10,11},{13,12},{14,15},{17,16},{18,... | collective-permute-start | bytes 1572872 | tf_op jit(solution)/shard_map/ppermute | solution.py:61
  352.2 22.5 %collective-permute-start.11 = (f32[256,512]{1,0:T(8,128)S(1)}, f32[256,512]{1,0:T(8,128)S(1)}, u32[]{:S(2)}, u32[]{:S(2)}) collective-permute-start(f32[256,512]{1,0:T(8,128)S(1)} %slice_add_fusion.5), channel_id=1, source_target_pairs={{1,0},{2,3},{5,4},{6,7},{9,8},{10,11},{13,12},{14,15},{17,16},{18,... | collective-permute-start | bytes 1572872 | tf_op jit(solution)/shard_map/ppermute | solution.py:61
  363.4 19.4 %collective-permute-start.19 = (f32[256,512]{1,0:T(8,128)S(1)}, f32[256,512]{1,0:T(8,128)S(1)}, u32[]{:S(2)}, u32[]{:S(2)}) collective-permute-start(f32[256,512]{1,0:T(8,128)S(1)} %slice_add_fusion.3), channel_id=1, source_target_pairs={{1,0},{2,3},{5,4},{6,7},{9,8},{10,11},{13,12},{14,15},{17,16},{18,... | collective-permute-start | bytes 1572872 | tf_op jit(solution)/shard_map/ppermute | solution.py:61
  374.6 13.9 %collective-permute-start.4 = (f32[128,512]{1,0:T(8,128)S(1)}, f32[128,512]{1,0:T(8,128)S(1)}, u32[]{:S(2)}, u32[]{:S(2)}) collective-permute-start(f32[128,512]{1,0:T(8,128)S(1)} %dynamic-slice_bitcast_fusion.7), channel_id=1, source_target_pairs={{0,8},{8,0},{1,9},{9,1},{2,10},{10,2},{3,11},{11,3},{4,12},{12,4},... | collective-permute-start | bytes 786440 | tf_op jit(solution)/shard_map/ppermute | solution.py:69
  376.7 12.5 %collective-permute-start.8 = (f32[128,512]{1,0:T(8,128)S(1)}, f32[128,512]{1,0:T(8,128)S(1)}, u32[]{:S(2)}, u32[]{:S(2)}) collective-permute-start(f32[128,512]{1,0:T(8,128)S(1)} %dynamic-slice_bitcast_fusion.6), channel_id=1, source_target_pairs={{0,8},{8,0},{1,9},{9,1},{2,10},{10,2},{3,11},{11,3},{4,12},{12,4},... | collective-permute-start | bytes 786440 | tf_op jit(solution)/shard_map/ppermute | solution.py:69
  382.8 9.2 %collective-permute-start.12 = (f32[128,512]{1,0:T(8,128)S(1)}, f32[128,512]{1,0:T(8,128)S(1)}, u32[]{:S(2)}, u32[]{:S(2)}) collective-permute-start(f32[128,512]{1,0:T(8,128)S(1)} %dynamic-slice_bitcast_fusion.5), channel_id=1, source_target_pairs={{0,8},{8,0},{1,9},{9,1},{2,10},{10,2},{3,11},{11,3},{4,12},{12,4},... | collective-permute-start | bytes 786440 | tf_op jit(solution)/shard_map/ppermute | solution.py:69
  384.9 12.7 %collective-permute-start.16 = (f32[128,512]{1,0:T(8,128)S(1)}, f32[128,512]{1,0:T(8,128)S(1)}, u32[]{:S(2)}, u32[]{:S(2)}) collective-permute-start(f32[128,512]{1,0:T(8,128)S(1)} %dynamic-slice_bitcast_fusion.4), channel_id=1, source_target_pairs={{0,8},{8,0},{1,9},{9,1},{2,10},{10,2},{3,11},{11,3},{4,12},{12,4},... | collective-permute-start | bytes 786440 | tf_op jit(solution)/shard_map/ppermute | solution.py:69
  386.0 17.2 %collective-permute-start.20 = (f32[128,512]{1,0:T(8,128)S(1)}, f32[128,512]{1,0:T(8,128)S(1)}, u32[]{:S(2)}, u32[]{:S(2)}) collective-permute-start(f32[128,512]{1,0:T(8,128)S(1)} %dynamic-slice_bitcast_fusion.3), channel_id=1, source_target_pairs={{0,8},{8,0},{1,9},{9,1},{2,10},{10,2},{3,11},{11,3},{4,12},{12,4},... | collective-permute-start | bytes 786440 | tf_op jit(solution)/shard_map/ppermute | solution.py:69
  388.5 20.3 %collective-permute-start.24 = (f32[128,512]{1,0:T(8,128)S(1)}, f32[128,512]{1,0:T(8,128)S(1)}, u32[]{:S(2)}, u32[]{:S(2)}) collective-permute-start(f32[128,512]{1,0:T(8,128)S(1)} %dynamic-slice_bitcast_fusion.2), channel_id=1, source_target_pairs={{0,8},{8,0},{1,9},{9,1},{2,10},{10,2},{3,11},{11,3},{4,12},{12,4},... | collective-permute-start | bytes 786440 | tf_op jit(solution)/shard_map/ppermute | solution.py:69
  389.2 25.2 %collective-permute-start.28 = (f32[128,512]{1,0:T(8,128)S(1)}, f32[128,512]{1,0:T(8,128)S(1)}, u32[]{:S(2)}, u32[]{:S(2)}) collective-permute-start(f32[128,512]{1,0:T(8,128)S(1)} %dynamic-slice_bitcast_fusion.1), channel_id=1, source_target_pairs={{0,8},{8,0},{1,9},{9,1},{2,10},{10,2},{3,11},{11,3},{4,12},{12,4},... | collective-permute-start | bytes 786440 | tf_op jit(solution)/shard_map/ppermute | solution.py:69
  392.0 25.6 %collective-permute-start.32 = (f32[128,512]{1,0:T(8,128)S(1)}, f32[128,512]{1,0:T(8,128)S(1)}, u32[]{:S(2)}, u32[]{:S(2)}) collective-permute-start(f32[128,512]{1,0:T(8,128)S(1)} %dynamic-slice_bitcast_fusion), channel_id=1, source_target_pairs={{0,8},{8,0},{1,9},{9,1},{2,10},{10,2},{3,11},{11,3},{4,12},{12,4},... | collective-permute-start | bytes 786440 | tf_op jit(solution)/shard_map/ppermute | solution.py:69
  414.5 3.0 copy-start
Sparse Core Ops, SparseCore 0:
  13.9 35.8 all-gather.2
  51.3 33.0 all-gather.4
